TPU v7x, 512 devices: a whole 4x8x8 slice. The times are simulated.
512 devices in a mesh: expert: 64 (over y, z_hi, core), narrow: 8 (over z_lo, x).
Axes of the slice: x: 4, y: 8, z: 8 (z_hi: 4, z_lo: 2; z = z_hi * 2 + z_lo), core: 2. Of those that a mesh axis runs over, the one named last changes fastest.
Arguments:
- tokens: bfloat16 [3072, 4096], P('expert', 'narrow'), may hold values from -6 to 6
- route_ids: int32 [3072, 8], P('expert'), may hold values from 0 to 63, all different within a row; in each aligned block of 48 rows (0 to 47, 48 to 95, ...) at most 12 rows name the same one
- route_weight: bfloat16 [3072, 8], P('expert'), may hold values from 0.049804688 to 0.5
- partner: int32 [64], replicated, may hold values from 0 to 63, as said below
- old_place: int32 [64], replicated, may hold values from 0 to 63, each once
- gate_weight: bfloat16 [64, 768, 4096], P('expert', 'narrow'), may hold values from -0.09375 to 0.09375
- up_weight: bfloat16 [64, 768, 4096], P('expert', 'narrow'), may hold values from -0.09375 to 0.09375
- down_weight: bfloat16 [64, 768, 4096], P('expert', None, 'narrow'), may hold values from -0.21875 to 0.21875
Outputs:
- layer_out: bfloat16 [3072, 4096], P('expert', 'narrow')
- new_gate: bfloat16 [64, 768, 4096], P('expert', 'narrow')
- new_up: bfloat16 [64, 768, 4096], P('expert', 'narrow')
- new_down: bfloat16 [64, 768, 4096], P('expert', None, 'narrow')
Inputs may be any that keep to these rules, and one draw needn't show every extreme that they name: partner[partner[s]] == s for every slot; slots with partner[s] == s keep their weights; the number of pairs varies between draws from 1 to 32. `old_place`: a permutation of the experts. `route_ids`: each row names 8 different experts; among the 48 tokens of one index of expert, no expert is named by more than 12 tokens.
All inputs are finite; a program needn't handle non-finite values.
Results may differ from a plain program's by a relative error of at most 0.0058.
Values may be sent and summed in bfloat16 or wider, within the bound.
No kernel may reach another device: no remote copies, remote signals or barrier semaphores. Data moves between devices by JAX's collectives and lax.ppermute only.
A program may use at most 128 MiB of HBM per device.

v0:
```python
import jax
import jax.numpy as jnp
from jax import lax
from jax.sharding import PartitionSpec as P


def slot_layout(route_ids, route_weight, holder, groups):
    tokens_here, top_count = route_ids.shape
    capacity = 2 * tokens_here * top_count // groups
    slot_ids = jnp.arange(groups, dtype=jnp.int32)
    matches = (holder[None, None, :] == route_ids[:, :, None]).astype(jnp.int32)
    target = jnp.sum(matches * slot_ids[None, None, :], axis=2)
    onehot = matches.reshape(tokens_here * top_count, groups)
    running = jnp.cumsum(onehot, axis=0) - 1
    position = jnp.sum(onehot * running, axis=1).reshape(tokens_here, top_count)
    row_index = target * capacity + position
    buffer_rows = jnp.arange(groups * capacity, dtype=jnp.int32)
    row_hits = buffer_rows[:, None, None] == row_index[None, :, :]
    dispatch = jnp.sum(row_hits.astype(jnp.float32), axis=2).astype(jnp.bfloat16)
    token_hits = row_index[:, :, None] == buffer_rows[None, None, :]
    combine = jnp.sum(
        jnp.where(token_hits, route_weight[:, :, None], jnp.zeros((), jnp.bfloat16)), axis=1
    )
    return (dispatch, combine, capacity)


def contract_last(left, right):
    return lax.dot_general(
        left, right, (((1,), (1,)), ((), ())), preferred_element_type=jnp.float32
    )


def body(tokens, route_ids, route_weight, partner, old_place, gate_weight, up_weight, down_weight):
    groups = lax.axis_size("expert")
    gate_flat = gate_weight.reshape(groups, -1)
    up_flat = up_weight.reshape(groups, -1)
    down_flat = down_weight.reshape(groups, -1)
    spread = (
        lax.all_to_all(gate_flat, "expert", split_axis=0, concat_axis=0, tiled=True),
        lax.all_to_all(up_flat, "expert", split_axis=0, concat_axis=0, tiled=True),
        lax.all_to_all(down_flat, "expert", split_axis=0, concat_axis=0, tiled=True),
    )
    gate_order = jnp.take(spread[0], partner, axis=0)
    up_order = jnp.take(spread[1], partner, axis=0)
    down_order = jnp.take(spread[2], partner, axis=0)
    arrived = (
        lax.all_to_all(gate_order, "expert", split_axis=0, concat_axis=0, tiled=True),
        lax.all_to_all(up_order, "expert", split_axis=0, concat_axis=0, tiled=True),
        lax.all_to_all(down_order, "expert", split_axis=0, concat_axis=0, tiled=True),
    )
    new_gate = arrived[0].reshape(gate_weight.shape)
    new_up = arrived[1].reshape(up_weight.shape)
    new_down = arrived[2].reshape(down_weight.shape)
    holder = jnp.take(old_place, partner)
    gate_block = new_gate[0]
    up_block = new_up[0]
    down_block = new_down[0]
    dispatch, combine, capacity = slot_layout(route_ids, route_weight, holder, groups)
    full_tokens = lax.all_gather(tokens, "narrow", axis=1, tiled=True)
    outgoing = jnp.dot(dispatch, full_tokens, preferred_element_type=jnp.float32).astype(
        jnp.bfloat16
    )
    arrived_rows = lax.all_to_all(
        outgoing.reshape(groups, capacity, -1), "expert", split_axis=0, concat_axis=0, tiled=True
    )
    flat_rows = arrived_rows.reshape(-1, arrived_rows.shape[2])
    gate_sum = contract_last(flat_rows, gate_block)
    up_sum = contract_last(flat_rows, up_block)
    hidden = (jax.nn.silu(gate_sum) * up_sum).astype(jnp.bfloat16)
    produced = (
        jnp.dot(
            lax.all_gather(hidden, "narrow", axis=1, tiled=True),
            down_block,
            preferred_element_type=jnp.float32,
        )
        .astype(jnp.bfloat16)
        .reshape(arrived_rows.shape[0], arrived_rows.shape[1], -1)
    )
    returned = lax.all_to_all(produced, "expert", split_axis=0, concat_axis=0, tiled=True)
    layer_out = jnp.dot(
        combine, returned.reshape(-1, returned.shape[2]), preferred_element_type=jnp.float32
    ).astype(jnp.bfloat16)
    return (layer_out, new_gate, new_up, new_down)


def solution(mesh):
    return jax.shard_map(
        body,
        mesh=mesh,
        in_specs=(
            P("expert", "narrow"),
            P("expert", None),
            P("expert", None),
            P(),
            P(),
            P("expert", "narrow", None),
            P("expert", "narrow", None),
            P("expert", None, "narrow"),
        ),
        out_specs=(
            P("expert", "narrow"),
            P("expert", "narrow", None),
            P("expert", "narrow", None),
            P("expert", None, "narrow"),
        ),
        check_vma=False,
    )
```

profile of v0, /device:TPU:80, one launch (start us, length us, event | category | flops | bytes accessed | tf_op | source)
XLA Modules:
  0.0 634.3 jit_solution(16042910142443403601)
XLA Ops:
  7.2 4.7 all_to_all.67
  12.4 5.5 reduce.9
  19.4 16.0 %all-to-all-start.5 = ((bf16[64,2,3072]{2,1,0:T(2,128)(2,1)}), bf16[64,2,3072]{2,1,0:T(2,128)(2,1)S(1)}, u32[]{:S(2)}, u32[]{:S(2)}) async-start(bf16[64,2,3072]{2,1,0:T(2,128)(2,1)} %reshape.175), calls=%async_computation.5 | async-start | bytes 1572864 | tf_op jit(solution)/shard_map/all_to_all | solution.py:41
  36.7 5.5 reduce.10
  43.6 17.1 %all-to-all-done.5 = bf16[64,2,3072]{2,1,0:T(2,128)(2,1)S(1)} async-done(((bf16[64,2,3072]{2,1,0:T(2,128)(2,1)}), bf16[64,2,3072]{2,1,0:T(2,128)(2,1)S(1)}, u32[]{:S(2)}, u32[]{:S(2)}) %all-to-all-start.5) | async-done | bytes 786464 | tf_op jit(solution)/shard_map/all_to_all | solution.py:41
  60.7 6.1 all-to-all-start.1
  68.1 5.5 reduce.11
  75.1 16.9 %all-to-all-done.1 = bf16[64,2,3072]{2,1,0:T(2,128)(2,1)} async-done(((bf16[64,2,3072]{2,1,0:T(2,128)(2,1)}), bf16[64,2,3072]{2,1,0:T(2,128)(2,1)}, u32[]{:S(2)}, u32[]{:S(2)}) %all-to-all-start.1) | async-done | bytes 786464 | tf_op jit(solution)/shard_map/all_to_all | solution.py:39
  92.0 6.3 all-to-all-start.3
  101.3 4.9 reshape.172
  108.6 15.0 %all-to-all-done.3 = bf16[64,2,3072]{2,1,0:T(2,128)(2,1)} async-done(((bf16[64,2,3072]{2,1,0:T(2,128)(2,1)}), bf16[64,2,3072]{2,1,0:T(2,128)(2,1)}, u32[]{:S(2)}, u32[]{:S(2)}) %all-to-all-start.3) | async-done | bytes 786464 | tf_op jit(solution)/shard_map/all_to_all | solution.py:40
  123.6 4.9 reshape.168
  131.5 2.3 reduce.12
  135.2 5.5 all-to-all-start.4
  143.4 22.8 %all-to-all-done.4 = bf16[64,2,3072]{2,1,0:T(2,128)(2,1)S(1)} async-done(((bf16[64,2,3072]{2,1,0:T(2,128)(2,1)}), bf16[64,2,3072]{2,1,0:T(2,128)(2,1)S(1)}, u32[]{:S(2)}, u32[]{:S(2)}) %all-to-all-start.4) | async-done | bytes 786464 | tf_op jit(solution)/shard_map/all_to_all | solution.py:48
  166.3 5.5 all-to-all-start.2
  175.0 37.4 %all_gather.6 = bf16[48,4096]{1,0:T(8,128)(2,1)S(1)} all-gather(bf16[48,512]{1,0:T(8,128)(2,1)S(1)} %copy-done.10), channel_id=1, replica_groups=mesh['expert'=64,'narrow'=8] {'narrow'}, dimensions={1}, use_global_device_ids=true | all-gather | bytes 442368 | tf_op jit(solution)/shard_map/all_gather | solution.py:59
  212.3 4.5 convolution_convert_fusion
  216.8 9.7 %reshape.111 = bf16[64,12,4096]{2,1,0:T(8,128)(2,1)} reshape(bf16[768,4096]{1,0:T(8,128)(2,1)} %convolution_convert_fusion) | data formatting | bytes 12582912 | tf_op jit(solution)/shard_map/reshape | solution.py:64
  227.4 15.7 %all-to-all-start = ((bf16[64,12,4096]{2,1,0:T(8,128)(2,1)}), bf16[64,12,4096]{2,1,0:T(8,128)(2,1)}, u32[]{:S(2)}, u32[]{:S(2)}) async-start(bf16[64,12,4096]{2,1,0:T(8,128)(2,1)} %reshape.111), calls=%async_computation | async-start | bytes 16777216 | tf_op jit(solution)/shard_map/all_to_all | solution.py:63
  243.8 4.9 reduce.3
  250.8 4.9 reduce.2
  256.3 206.2 %all-to-all-done = bf16[64,12,4096]{2,1,0:T(8,128)(2,1)} async-done(((bf16[64,12,4096]{2,1,0:T(8,128)(2,1)}), bf16[64,12,4096]{2,1,0:T(8,128)(2,1)}, u32[]{:S(2)}, u32[]{:S(2)}) %all-to-all-start) | async-done | bytes 6291488 | tf_op jit(solution)/shard_map/all_to_all | solution.py:63
  462.5 10.0 %reshape.112 = bf16[768,4096]{1,0:T(8,128)(2,1)} reshape(bf16[64,12,4096]{2,1,0:T(8,128)(2,1)} %all-to-all-done) | data formatting | bytes 12582912 | tf_op jit(solution)/shard_map/reshape | solution.py:66
  472.5 5.0 fusion.6
  477.6 2.7 fusion.1
  482.1 54.6 %all_to_all.76 = bf16[64,2,3072]{2,1,0:T(2,128)(2,1)S(1)} all-to-all(bf16[64,2,3072]{2,1,0:T(2,128)(2,1)S(1)} %reshape.177), channel_id=1, replica_groups=mesh['expert'=64,'narrow'=8] {'expert'}, dimensions={0} | all-to-all | bytes 1572864 | tf_op jit(solution)/shard_map/all_to_all | solution.py:49
  538.7 5.8 reduce.4
  546.4 29.8 %all-gather.2.cloned.1.call-done = bf16[768,768]{0,1:T(8,128)(2,1)} async-done(((bf16[768,96]{0,1:T(8,128)(2,1)}), bf16[768,768]{0,1:T(8,128)(2,1)}) %all-gather.2.cloned.1.call-update) | async-done | bytes 1179664 | tf_op jit(solution)/shard_map/all_gather | solution.py:72
  576.2 2.3 convolution_convert_fusion.1
  579.7 15.6 %all-to-all-start.7 = ((bf16[64,12,512]{2,1,0:T(8,128)(2,1)}), bf16[64,12,512]{2,1,0:T(8,128)(2,1)S(1)}, u32[]{:S(2)}, u32[]{:S(2)}) async-start(bf16[64,12,512]{2,1,0:T(8,128)(2,1)} %reshape.113), calls=%async_computation.7 | async-start | bytes 2097152 | tf_op jit(solution)/shard_map/all_to_all | solution.py:79
  600.6 25.5 %all-to-all-done.7 = bf16[64,12,512]{2,1,0:T(8,128)(2,1)S(1)} async-done(((bf16[64,12,512]{2,1,0:T(8,128)(2,1)}), bf16[64,12,512]{2,1,0:T(8,128)(2,1)S(1)}, u32[]{:S(2)}, u32[]{:S(2)}) %all-to-all-start.7) | async-done | bytes 786464 | tf_op jit(solution)/shard_map/all_to_all | solution.py:79
  (80 shorter events, 40.3 us)
Async XLA Ops:
  7.2 91.2 %copy-start = (s32[64]{0:T(128)S(1)}, s32[64]{0:T(128)}, u32[]{:S(2)}) copy-start(s32[64]{0:T(128)} %param.14) | copy-start | bytes 772
  19.4 16.0 %copy-start.8 = (bf16[1,96,4096]{2,1,0:T(8,128)(2,1)S(1)}, bf16[1,96,4096]{2,1,0:T(8,128)(2,1)}, u32[]{:S(2)}) copy-start(bf16[1,96,4096]{2,1,0:T(8,128)(2,1)} %param.15) | copy-start | bytes 2359300
  19.4 41.3 %all-to-all-start.5 = ((bf16[64,2,3072]{2,1,0:T(2,128)(2,1)}), bf16[64,2,3072]{2,1,0:T(2,128)(2,1)S(1)}, u32[]{:S(2)}, u32[]{:S(2)}) async-start(bf16[64,2,3072]{2,1,0:T(2,128)(2,1)} %reshape.175), calls=%async_computation.5 | async-start | bytes 1572864 | tf_op jit(solution)/shard_map/all_to_all | solution.py:41
  43.6 23.2 %copy-start.9 = (bf16[1,96,4096]{2,1,0:T(8,128)(2,1)S(1)}, bf16[1,96,4096]{2,1,0:T(8,128)(2,1)}, u32[]{:S(2)}) copy-start(bf16[1,96,4096]{2,1,0:T(8,128)(2,1)} %param.16) | copy-start | bytes 2359300
  60.7 31.3 %all-to-all-start.1 = ((bf16[64,2,3072]{2,1,0:T(2,128)(2,1)}), bf16[64,2,3072]{2,1,0:T(2,128)(2,1)}, u32[]{:S(2)}, u32[]{:S(2)}) async-start(bf16[64,2,3072]{2,1,0:T(2,128)(2,1)} %reshape.171), calls=%async_computation.1 | async-start | bytes 1572864 | tf_op jit(solution)/shard_map/all_to_all | solution.py:39
  73.6 24.7 %copy-start.13 = (s32[64]{0:T(128)S(1)}, s32[64]{0:T(128)}, u32[]{:S(2)}) copy-start(s32[64]{0:T(128)} %param.13) | copy-start | bytes 772
  92.0 31.5 %all-to-all-start.3 = ((bf16[64,2,3072]{2,1,0:T(2,128)(2,1)}), bf16[64,2,3072]{2,1,0:T(2,128)(2,1)}, u32[]{:S(2)}, u32[]{:S(2)}) async-start(bf16[64,2,3072]{2,1,0:T(2,128)(2,1)} %reshape.167), calls=%async_computation.3 | async-start | bytes 1572864 | tf_op jit(solution)/shard_map/all_to_all | solution.py:40
  128.9 1.1 copy-start.3
  135.2 31.0 %all-to-all-start.4 = ((bf16[64,2,3072]{2,1,0:T(2,128)(2,1)}), bf16[64,2,3072]{2,1,0:T(2,128)(2,1)S(1)}, u32[]{:S(2)}, u32[]{:S(2)}) async-start(bf16[64,2,3072]{2,1,0:T(2,128)(2,1)} %reshape.169), calls=%async_computation.4 | async-start | bytes 1572864 | tf_op jit(solution)/shard_map/all_to_all | solution.py:48
  142.0 29.8 %copy-start.11 = (s32[48,8]{0,1:T(8,128)S(1)}, s32[48,8]{0,1:T(8,128)}, u32[]{:S(2)}) copy-start(s32[48,8]{0,1:T(8,128)} %param.11) | copy-start | bytes 4612
  143.4 31.5 %copy-start.10 = (bf16[48,512]{1,0:T(8,128)(2,1)S(1)}, bf16[48,512]{1,0:T(8,128)(2,1)}, u32[]{:S(2)}) copy-start(bf16[48,512]{1,0:T(8,128)(2,1)} %param.10) | copy-start | bytes 147460
  166.3 60.3 %all-to-all-start.2 = ((bf16[64,2,3072]{2,1,0:T(2,128)(2,1)}), bf16[64,2,3072]{2,1,0:T(2,128)(2,1)S(1)}, u32[]{:S(2)}, u32[]{:S(2)}) async-start(bf16[64,2,3072]{2,1,0:T(2,128)(2,1)} %reshape.173), calls=%async_computation.2 | async-start | bytes 1572864 | tf_op jit(solution)/shard_map/all_to_all | solution.py:47
  226.6 0.9 copy-start.5
  227.4 235.0 %all-to-all-start = ((bf16[64,12,4096]{2,1,0:T(8,128)(2,1)}), bf16[64,12,4096]{2,1,0:T(8,128)(2,1)}, u32[]{:S(2)}, u32[]{:S(2)}) async-start(bf16[64,12,4096]{2,1,0:T(8,128)(2,1)} %reshape.111), calls=%async_computation | async-start | bytes 16777216 | tf_op jit(solution)/shard_map/all_to_all | solution.py:63
  243.1 333.1 %all-gather.2.cloned.1.call-start = ((), (), s32[]{:S(2)}) async-start(), calls=%async_computation.8 | async-start | bytes 1327104 | tf_op jit(solution)/shard_map/all_gather | solution.py:72
  248.7 1.5 copy-start.6
  472.5 5.0 copy-start.2
  472.5 5.0 copy-start.7
  477.6 2.8 copy-start.4
  578.5 16.8 %copy-start.12 = (bf16[48,8]{0,1:T(8,128)(2,1)S(1)}, bf16[48,8]{0,1:T(8,128)(2,1)}, u32[]{:S(2)}) copy-start(bf16[48,8]{0,1:T(8,128)(2,1)} %param.12) | copy-start | bytes 2308
  579.7 46.5 %all-to-all-start.7 = ((bf16[64,12,512]{2,1,0:T(8,128)(2,1)}), bf16[64,12,512]{2,1,0:T(8,128)(2,1)S(1)}, u32[]{:S(2)}, u32[]{:S(2)}) async-start(bf16[64,12,512]{2,1,0:T(8,128)(2,1)} %reshape.113), calls=%async_computation.7 | async-start | bytes 2097152 | tf_op jit(solution)/shard_map/all_to_all | solution.py:79
  598.8 28.4 %copy-start.1 = (s32[64]{0:T(128)S(1)}, s32[64]{0:T(128)}, u32[]{:S(2)}) copy-start(s32[64]{0:T(128)} %param.14) | copy-start | bytes 772
Sparse Core Ops, SparseCore 0:
  480.5 95.6 all-gather.1
where the time goes:
time: 641 us; the launch traced here: 634 us
  waiting for transfers between devices  333 us (52%)
  blocking collectives  92 us (14%)
  starting transfers between devices  70.7 us (11%)
  local copies, waits for them, and re-layouts  66.9 us (10%)
  other arithmetic  41.2 us (6%)
  matrix products  15.4 us (2%)
  between operations  14.8 us (2%)
    all_to_all x1, waiting for transfers between devices, body(): lax.all_to_all(outgoing.reshape(groups, capacity, -1), 'expert', split_ax...  206 us
    all_to_all x1, blocking collectives, body(): lax.all_to_all(down_order, 'expert', split_axis=0, concat_axis=0, tiled=T...  54.6 us
    all_gather x1, blocking collectives, body(): full_tokens = lax.all_gather(tokens, 'narrow', axis=1, tiled=True)  37.4 us
    all_gather x1, waiting for transfers between devices, body(): lax.all_gather(hidden, 'narrow', axis=1, tiled=True)  29.8 us
    all_to_all x1, waiting for transfers between devices, body(): lax.all_to_all(produced, 'expert', split_axis=0, concat_axis=0, tiled=True)  25.5 us
    unnamed x45, local copies, waits for them, and re-layouts  24.1 us
    all_to_all x1, waiting for transfers between devices, body(): lax.all_to_all(up_order, 'expert', split_axis=0, concat_axis=0, tiled=True)  22.8 us
    all_to_all x1, waiting for transfers between devices, body(): lax.all_to_all(down_flat, 'expert', split_axis=0, concat_axis=0, tiled=True)  17.1 us
  transfers between devices with their start and end apart: 8, of which 7 were waited for; matrix products, arithmetic and copies ran while one was open for 12% of the time, Pallas kernels for 0%

commit v1 on v0

--- a/solution.py
+++ b/solution.py
@@ -2,6 +2,11 @@
 import jax.numpy as jnp
 from jax import lax
 from jax.sharding import PartitionSpec as P
+
+
+def all_by_exchange(array, axis, along):
+    sent = jnp.stack([array] * lax.axis_size(axis))
+    return jnp.concatenate(lax.all_to_all(sent, axis, 0, 0), axis=along)
 
 
 def slot_layout(route_ids, route_weight, holder, groups):
@@ -56,7 +61,7 @@
     up_block = new_up[0]
     down_block = new_down[0]
     dispatch, combine, capacity = slot_layout(route_ids, route_weight, holder, groups)
-    full_tokens = lax.all_gather(tokens, "narrow", axis=1, tiled=True)
+    full_tokens = all_by_exchange(tokens, "narrow", 1)
     outgoing = jnp.dot(dispatch, full_tokens, preferred_element_type=jnp.float32).astype(
         jnp.bfloat16
     )

time: 641 us -> 604 us (0.942)
  blocking collectives: 92 us -> 45.7 us
  waiting for transfers between devices: 333 us -> 346 us
    all_gather x1 -> x0, blocking collectives: 37.4 us -> none  [body(): full_tokens = lax.all_gather(tokens, 'narrow', axis=1, tiled=True)]
    all_to_all x1, starting transfers between devices: 15.7 us -> 5.74 us  [body(): lax.all_to_all(outgoing.reshape(groups, capacity, -1), 'expert', split_ax...]
    all_to_all x1, blocking collectives: 54.6 us -> 45.7 us  [body(): lax.all_to_all(down_order, 'expert', split_axis=0, concat_axis=0, tiled=T...]
    all_to_all x1, waiting for transfers between devices: 0.01 us -> 7.88 us  [body(): lax.all_to_all(gate_order, 'expert', split_axis=0, concat_axis=0, tiled=T...]
    all_to_all x1, waiting for transfers between devices: 206 us -> 214 us  [body(): lax.all_to_all(outgoing.reshape(groups, capacity, -1), 'expert', split_ax...]
    unnamed x45 -> x49, local copies, waits for them, and re-layouts: 24.1 us -> 24.3 us
  transfers between devices with their start and end apart: 8 -> 9, of which waited for: 7 -> 8; matrix products, arithmetic and copies ran while one was open for 12% -> 14% of each run, Pallas kernels for 0% -> 0%
where the time goes in v1:
time: 604 us; the launch traced here: 597 us
  waiting for transfers between devices  346 us (57%)
  local copies, waits for them, and re-layouts  67.9 us (11%)
  starting transfers between devices  66.6 us (11%)
  blocking collectives  45.7 us (8%)
  other arithmetic  40.6 us (7%)
  matrix products  15.4 us (3%)
  between operations  14.8 us (2%)
    all_to_all x1, waiting for transfers between devices, body(): lax.all_to_all(outgoing.reshape(groups, capacity, -1), 'expert', split_ax...  214 us
    all_to_all x1, blocking collectives, body(): lax.all_to_all(down_order, 'expert', split_axis=0, concat_axis=0, tiled=T...  45.7 us
    all_gather x1, waiting for transfers between devices, body(): lax.all_gather(hidden, 'narrow', axis=1, tiled=True)  26.9 us
    all_to_all x1, waiting for transfers between devices, body(): lax.all_to_all(produced, 'expert', split_axis=0, concat_axis=0, tiled=True)  25.5 us
    unnamed x49, local copies, waits for them, and re-layouts  24.3 us
    all_to_all x1, waiting for transfers between devices, body(): lax.all_to_all(up_order, 'expert', split_axis=0, concat_axis=0, tiled=True)  22.9 us
    all_to_all x1, waiting for transfers between devices, body(): lax.all_to_all(down_flat, 'expert', split_axis=0, concat_axis=0, tiled=True)  17.1 us
    all_to_all x1, waiting for transfers between devices, body(): lax.all_to_all(gate_flat, 'expert', split_axis=0, concat_axis=0, tiled=True)  17 us
  transfers between devices with their start and end apart: 9, of which 8 were waited for; matrix products, arithmetic and copies ran while one was open for 14% of the time, Pallas kernels for 0%

profile of v1, /device:TPU:80, one launch (start us, length us, event | category | flops | bytes accessed | tf_op | source)
XLA Modules:
  0.0 597.1 jit_solution(8275535595310786972)
XLA Ops:
  7.2 4.7 all_to_all.71
  12.4 5.4 reduce.9
  19.3 16.0 %all-to-all-start.6 = ((bf16[64,2,3072]{2,1,0:T(2,128)(2,1)}), bf16[64,2,3072]{2,1,0:T(2,128)(2,1)S(1)}, u32[]{:S(2)}, u32[]{:S(2)}) async-start(bf16[64,2,3072]{2,1,0:T(2,128)(2,1)} %reshape.185), calls=%async_computation.6 | async-start | bytes 1572864 | tf_op jit(solution)/shard_map/all_to_all | solution.py:46
  36.6 5.4 reduce.10
  43.5 17.1 %all-to-all-done.6 = bf16[64,2,3072]{2,1,0:T(2,128)(2,1)S(1)} async-done(((bf16[64,2,3072]{2,1,0:T(2,128)(2,1)}), bf16[64,2,3072]{2,1,0:T(2,128)(2,1)S(1)}, u32[]{:S(2)}, u32[]{:S(2)}) %all-to-all-start.6) | async-done | bytes 786464 | tf_op jit(solution)/shard_map/all_to_all | solution.py:46
  60.6 6.1 %all-to-all-start.2 = ((bf16[64,2,3072]{2,1,0:T(2,128)(2,1)}), bf16[64,2,3072]{2,1,0:T(2,128)(2,1)}, u32[]{:S(2)}, u32[]{:S(2)}) async-start(bf16[64,2,3072]{2,1,0:T(2,128)(2,1)} %reshape.181), calls=%async_computation.2 | async-start | bytes 1572864 | tf_op jit(solution)/shard_map/all_to_all | solution.py:44
  68.0 5.4 reduce.11
  74.9 17.0 %all-to-all-done.2 = bf16[64,2,3072]{2,1,0:T(2,128)(2,1)} async-done(((bf16[64,2,3072]{2,1,0:T(2,128)(2,1)}), bf16[64,2,3072]{2,1,0:T(2,128)(2,1)}, u32[]{:S(2)}, u32[]{:S(2)}) %all-to-all-start.2) | async-done | bytes 786464 | tf_op jit(solution)/shard_map/all_to_all | solution.py:44
  91.9 5.7 all-to-all-start.4
  100.6 4.9 reshape.182
  107.9 15.2 %all-to-all-done.4 = bf16[64,2,3072]{2,1,0:T(2,128)(2,1)} async-done(((bf16[64,2,3072]{2,1,0:T(2,128)(2,1)}), bf16[64,2,3072]{2,1,0:T(2,128)(2,1)}, u32[]{:S(2)}, u32[]{:S(2)}) %all-to-all-start.4) | async-done | bytes 786464 | tf_op jit(solution)/shard_map/all_to_all | solution.py:45
  123.8 6.2 %all-to-all-start = ((bf16[8,48,512]{2,1,0:T(8,128)(2,1)}), bf16[8,48,512]{2,1,0:T(8,128)(2,1)S(1)}, u32[]{:S(2)}, u32[]{:S(2)}) async-start(bf16[8,48,512]{2,1,0:T(8,128)(2,1)} %stack.2), calls=%async_computation | async-start | bytes 786432 | tf_op jit(solution)/shard_map/all_to_all | solution.py:9
  130.0 4.9 reshape.178
  141.7 5.5 all-to-all-start.5
  149.8 22.9 %all-to-all-done.5 = bf16[64,2,3072]{2,1,0:T(2,128)(2,1)S(1)} async-done(((bf16[64,2,3072]{2,1,0:T(2,128)(2,1)}), bf16[64,2,3072]{2,1,0:T(2,128)(2,1)S(1)}, u32[]{:S(2)}, u32[]{:S(2)}) %all-to-all-start.5) | async-done | bytes 786464 | tf_op jit(solution)/shard_map/all_to_all | solution.py:53
  172.7 5.5 all-to-all-start.3
  181.6 4.5 convolution_convert_fusion
  186.1 9.7 %reshape.121 = bf16[64,12,4096]{2,1,0:T(8,128)(2,1)} reshape(bf16[768,4096]{1,0:T(8,128)(2,1)} %convolution_convert_fusion) | data formatting | bytes 12582912 | tf_op jit(solution)/shard_map/reshape | solution.py:69
  195.8 7.9 %all-to-all-done.3 = bf16[64,2,3072]{2,1,0:T(2,128)(2,1)S(1)} async-done(((bf16[64,2,3072]{2,1,0:T(2,128)(2,1)}), bf16[64,2,3072]{2,1,0:T(2,128)(2,1)S(1)}, u32[]{:S(2)}, u32[]{:S(2)}) %all-to-all-start.3) | async-done | bytes 786464 | tf_op jit(solution)/shard_map/all_to_all | solution.py:52
  204.6 5.7 all-to-all-start.1
  211.2 4.9 reduce.3
  218.2 4.9 reduce.2
  223.7 213.5 %all-to-all-done.1 = bf16[64,12,4096]{2,1,0:T(8,128)(2,1)} async-done(((bf16[64,12,4096]{2,1,0:T(8,128)(2,1)}), bf16[64,12,4096]{2,1,0:T(8,128)(2,1)}, u32[]{:S(2)}, u32[]{:S(2)}) %all-to-all-start.1) | async-done | bytes 6291488 | tf_op jit(solution)/shard_map/all_to_all | solution.py:68
  437.2 10.0 %reshape.122 = bf16[768,4096]{1,0:T(8,128)(2,1)} reshape(bf16[64,12,4096]{2,1,0:T(8,128)(2,1)} %all-to-all-done.1) | data formatting | bytes 12582912 | tf_op jit(solution)/shard_map/reshape | solution.py:71
  447.3 5.0 fusion.6
  452.3 2.7 fusion.1
  456.8 45.7 %all_to_all.81 = bf16[64,2,3072]{2,1,0:T(2,128)(2,1)S(1)} all-to-all(bf16[64,2,3072]{2,1,0:T(2,128)(2,1)S(1)} %reshape.187), channel_id=1, replica_groups=mesh['expert'=64,'narrow'=8] {'expert'}, dimensions={0} | all-to-all | bytes 1572864 | tf_op jit(solution)/shard_map/all_to_all | solution.py:54
  504.4 5.8 reduce.4
  512.0 26.9 %all-gather.2.cloned.1.call-done = bf16[768,768]{0,1:T(8,128)(2,1)} async-done(((bf16[768,96]{0,1:T(8,128)(2,1)}), bf16[768,768]{0,1:T(8,128)(2,1)}) %all-gather.2.cloned.1.call-update) | async-done | bytes 1179664 | tf_op jit(solution)/shard_map/all_gather | solution.py:77
  539.0 2.3 convolution_convert_fusion.1
  542.4 15.6 %all-to-all-start.8 = ((bf16[64,12,512]{2,1,0:T(8,128)(2,1)}), bf16[64,12,512]{2,1,0:T(8,128)(2,1)S(1)}, u32[]{:S(2)}, u32[]{:S(2)}) async-start(bf16[64,12,512]{2,1,0:T(8,128)(2,1)} %reshape.123), calls=%async_computation.8 | async-start | bytes 2097152 | tf_op jit(solution)/shard_map/all_to_all | solution.py:84
  563.4 25.5 %all-to-all-done.8 = bf16[64,12,512]{2,1,0:T(8,128)(2,1)S(1)} async-done(((bf16[64,12,512]{2,1,0:T(8,128)(2,1)}), bf16[64,12,512]{2,1,0:T(8,128)(2,1)S(1)}, u32[]{:S(2)}, u32[]{:S(2)}) %all-to-all-start.8) | async-done | bytes 786464 | tf_op jit(solution)/shard_map/all_to_all | solution.py:84
  (87 shorter events, 43.6 us)
Async XLA Ops:
  7.2 90.5 %copy-start = (s32[64]{0:T(128)S(1)}, s32[64]{0:T(128)}, u32[]{:S(2)}) copy-start(s32[64]{0:T(128)} %param.14) | copy-start | bytes 772
  19.3 16.0 %copy-start.8 = (bf16[1,96,4096]{2,1,0:T(8,128)(2,1)S(1)}, bf16[1,96,4096]{2,1,0:T(8,128)(2,1)}, u32[]{:S(2)}) copy-start(bf16[1,96,4096]{2,1,0:T(8,128)(2,1)} %param.15) | copy-start | bytes 2359300
  19.3 41.3 %all-to-all-start.6 = ((bf16[64,2,3072]{2,1,0:T(2,128)(2,1)}), bf16[64,2,3072]{2,1,0:T(2,128)(2,1)S(1)}, u32[]{:S(2)}, u32[]{:S(2)}) async-start(bf16[64,2,3072]{2,1,0:T(2,128)(2,1)} %reshape.185), calls=%async_computation.6 | async-start | bytes 1572864 | tf_op jit(solution)/shard_map/all_to_all | solution.py:46
  43.5 23.3 %copy-start.9 = (bf16[1,96,4096]{2,1,0:T(8,128)(2,1)S(1)}, bf16[1,96,4096]{2,1,0:T(8,128)(2,1)}, u32[]{:S(2)}) copy-start(bf16[1,96,4096]{2,1,0:T(8,128)(2,1)} %param.16) | copy-start | bytes 2359300
  60.6 31.3 %all-to-all-start.2 = ((bf16[64,2,3072]{2,1,0:T(2,128)(2,1)}), bf16[64,2,3072]{2,1,0:T(2,128)(2,1)}, u32[]{:S(2)}, u32[]{:S(2)}) async-start(bf16[64,2,3072]{2,1,0:T(2,128)(2,1)} %reshape.181), calls=%async_computation.2 | async-start | bytes 1572864 | tf_op jit(solution)/shard_map/all_to_all | solution.py:44
  73.5 24.2 %copy-start.15 = (s32[64]{0:T(128)S(1)}, s32[64]{0:T(128)}, u32[]{:S(2)}) copy-start(s32[64]{0:T(128)} %param.13) | copy-start | bytes 772
  91.9 31.1 %all-to-all-start.4 = ((bf16[64,2,3072]{2,1,0:T(2,128)(2,1)}), bf16[64,2,3072]{2,1,0:T(2,128)(2,1)}, u32[]{:S(2)}, u32[]{:S(2)}) async-start(bf16[64,2,3072]{2,1,0:T(2,128)(2,1)} %reshape.177), calls=%async_computation.4 | async-start | bytes 1572864 | tf_op jit(solution)/shard_map/all_to_all | solution.py:45
  106.0 17.1 %copy-start.12 = (bf16[48,512]{1,0:T(8,128)(2,1)S(1)}, bf16[48,512]{1,0:T(8,128)(2,1)}, u32[]{:S(2)}) copy-start(bf16[48,512]{1,0:T(8,128)(2,1)} %param.10) | copy-start | bytes 147460
  123.8 17.8 %all-to-all-start = ((bf16[8,48,512]{2,1,0:T(8,128)(2,1)}), bf16[8,48,512]{2,1,0:T(8,128)(2,1)S(1)}, u32[]{:S(2)}, u32[]{:S(2)}) async-start(bf16[8,48,512]{2,1,0:T(8,128)(2,1)} %stack.2), calls=%async_computation | async-start | bytes 786432 | tf_op jit(solution)/shard_map/all_to_all | solution.py:9
  135.4 1.1 copy-start.3
  141.7 31.0 %all-to-all-start.5 = ((bf16[64,2,3072]{2,1,0:T(2,128)(2,1)}), bf16[64,2,3072]{2,1,0:T(2,128)(2,1)S(1)}, u32[]{:S(2)}, u32[]{:S(2)}) async-start(bf16[64,2,3072]{2,1,0:T(2,128)(2,1)} %reshape.179), calls=%async_computation.5 | async-start | bytes 1572864 | tf_op jit(solution)/shard_map/all_to_all | solution.py:53
  148.3 29.9 %copy-start.13 = (s32[48,8]{0,1:T(8,128)S(1)}, s32[48,8]{0,1:T(8,128)}, u32[]{:S(2)}) copy-start(s32[48,8]{0,1:T(8,128)} %param.11) | copy-start | bytes 4612
  172.7 31.0 %all-to-all-start.3 = ((bf16[64,2,3072]{2,1,0:T(2,128)(2,1)}), bf16[64,2,3072]{2,1,0:T(2,128)(2,1)S(1)}, u32[]{:S(2)}, u32[]{:S(2)}) async-start(bf16[64,2,3072]{2,1,0:T(2,128)(2,1)} %reshape.183), calls=%async_computation.3 | async-start | bytes 1572864 | tf_op jit(solution)/shard_map/all_to_all | solution.py:52
  180.9 0.6 copy-start.10
  203.7 0.9 copy-start.5
  204.6 232.6 %all-to-all-start.1 = ((bf16[64,12,4096]{2,1,0:T(8,128)(2,1)}), bf16[64,12,4096]{2,1,0:T(8,128)(2,1)}, u32[]{:S(2)}, u32[]{:S(2)}) async-start(bf16[64,12,4096]{2,1,0:T(8,128)(2,1)} %reshape.121), calls=%async_computation.1 | async-start | bytes 16777216 | tf_op jit(solution)/shard_map/all_to_all | solution.py:68
  210.3 328.6 %all-gather.2.cloned.1.call-start = ((), (), s32[]{:S(2)}) async-start(), calls=%async_computation.9 | async-start | bytes 1327104 | tf_op jit(solution)/shard_map/all_gather | solution.py:77
  216.1 1.5 copy-start.6
  447.3 5.0 copy-start.2
  447.3 5.0 copy-start.7
  452.3 2.8 copy-start.4
  541.2 16.8 %copy-start.14 = (bf16[48,8]{0,1:T(8,128)(2,1)S(1)}, bf16[48,8]{0,1:T(8,128)(2,1)}, u32[]{:S(2)}) copy-start(bf16[48,8]{0,1:T(8,128)(2,1)} %param.12) | copy-start | bytes 2308
  541.3 16.9 %copy-start.11 = (s32[48,8]{1,0:T(8,128)S(1)}, s32[48,8]{1,0:T(8,128)}, u32[]{:S(2)}) copy-start(s32[48,8]{1,0:T(8,128)} %copy-done.10) | copy-start | bytes 4612
  542.4 46.5 %all-to-all-start.8 = ((bf16[64,12,512]{2,1,0:T(8,128)(2,1)}), bf16[64,12,512]{2,1,0:T(8,128)(2,1)S(1)}, u32[]{:S(2)}, u32[]{:S(2)}) async-start(bf16[64,12,512]{2,1,0:T(8,128)(2,1)} %reshape.123), calls=%async_computation.8 | async-start | bytes 2097152 | tf_op jit(solution)/shard_map/all_to_all | solution.py:84
  561.5 28.4 %copy-start.1 = (s32[64]{0:T(128)S(1)}, s32[64]{0:T(128)}, u32[]{:S(2)}) copy-start(s32[64]{0:T(128)} %param.14) | copy-start | bytes 772
Sparse Core Ops, SparseCore 0:
  455.2 83.6 all-gather.1
